TPU v7x, 256 devices: a whole 4x4x8 slice. The times are simulated.
256 devices in a mesh: gx: 32 (over z, x), gy: 8 (over y, core).
Axes of the slice: x: 4, y: 4, z: 8, core: 2. Of those that a mesh axis runs over, the one named last changes fastest.
Arguments:
- hidden_in: bfloat16 [64, 5120], P(None, 'gx'), may hold values from -60 to 60
- norm1_gain: float32 [5120], P('gx'), may hold values from 0.1 to 1.9
- norm1_bias: float32 [5120], P('gx'), may hold values from -4 to 4
- norm2_gain: float32 [5120], P('gx'), may hold values from 0.1 to 1.9
- norm2_bias: float32 [5120], P('gx'), may hold values from -4 to 4
- w_qkv: bfloat16 [5120, 15360], P('gx', 'gy'), may hold values from -0.078125 to 0.078125
- b_qkv: float32 [15360], P('gy'), may hold values from -4 to 4
- w_out: bfloat16 [5120, 5120], P('gy', 'gx'), may hold values from -0.078125 to 0.078125
- b_out: float32 [5120], P('gx'), may hold values from -4 to 4
- w_up: bfloat16 [5120, 20480], P('gx', 'gy'), may hold values from -0.078125 to 0.078125
- b_up: float32 [20480], P('gy'), may hold values from -4 to 4
- w_down: bfloat16 [20480, 5120], P('gy', 'gx'), may hold values from -0.0390625 to 0.0390625
- b_down: float32 [5120], P('gx'), may hold values from -4 to 4
- key_cache: bfloat16 [64, 40, 1024, 128], P('gx', 'gy'), may hold values from -70 to 70
- value_cache: bfloat16 [64, 40, 1024, 128], P('gx', 'gy'), may hold values from -6 to 6
- lengths: int32 [64], replicated, may hold values from 1 to 1024, 32768 in all
- assignment: int32 [64], replicated, may hold values from 0 to 63, each once
Outputs:
- hidden_out: bfloat16 [64, 5120], P(None, 'gx')
- new_keys: bfloat16 [64, 40, 1024, 128], P('gx', 'gy')
- new_values: bfloat16 [64, 40, 1024, 128], P('gx', 'gy')
Inputs may be any that keep to these rules, and one draw needn't show every extreme that they name: `lengths`: each request's length, the largest exactly 1024. `assignment`: a permutation: every slot holds exactly one request.
All inputs are finite; a program needn't handle non-finite values.
Results may differ from a plain program's by a relative error of at most 0.0068.
Values may be sent and summed in bfloat16 or wider, within the bound.
No kernel may reach another device: no remote copies, remote signals or barrier semaphores. Data moves between devices by JAX's collectives and lax.ppermute only.
A program may use at most 64 MiB of HBM per device.

v0:
```python
import jax
import jax.numpy as jnp
from jax import lax
from jax.sharding import PartitionSpec as P

D = 5120
HD = 128
ROT = 32


def rotate(tensor, position):
    half_rot = ROT // 2
    frequency = 10000.0 ** (-2.0 * jnp.arange(half_rot, dtype=jnp.float32) / ROT)
    angle = position.astype(jnp.float32)[:, None, None] * frequency
    cosine = jnp.cos(angle)
    sine = jnp.sin(angle)
    first_half = tensor[..., :half_rot]
    second_half = tensor[..., half_rot:ROT]
    return jnp.concatenate(
        [
            first_half * cosine - second_half * sine,
            second_half * cosine + first_half * sine,
            tensor[..., ROT:],
        ],
        axis=-1,
    )


def block_scores(query, keys, my_len):
    span_len = keys.shape[2]
    scores = jnp.einsum("shd,shpd->shp", query, keys, preferred_element_type=jnp.float32) * HD ** (
        -0.5
    )
    places = lax.iota(jnp.int32, span_len)
    valid = places[None, None, :] < my_len[:, None, None]
    return (jnp.where(valid, scores, -1e30), valid)


def on_device(
    hidden_in,
    norm1_gain,
    norm1_bias,
    norm2_gain,
    norm2_bias,
    w_qkv,
    b_qkv,
    w_out,
    b_out,
    w_up,
    b_up,
    w_down,
    b_down,
    key_cache,
    value_cache,
    lengths,
    assignment,
):
    requests = hidden_in.shape[0]
    rows_dev = key_cache.shape[0]
    heads_dev = key_cache.shape[1]
    wide_in = hidden_in.astype(jnp.float32)
    sum_rows, sum_squares = lax.psum(
        (jnp.sum(wide_in, axis=1), jnp.sum(wide_in * wide_in, axis=1)), "gx"
    )
    row_mean = sum_rows / D
    row_var = sum_squares / D - row_mean * row_mean
    normed = (wide_in - row_mean[:, None]) * lax.rsqrt(row_var + 1e-05)[:, None]
    attn_in = (normed * norm1_gain + norm1_bias).astype(jnp.bfloat16)
    mlp_in = (normed * norm2_gain + norm2_bias).astype(jnp.bfloat16)
    slot_ids = lax.iota(jnp.int32, requests)
    matches = assignment[:, None] == slot_ids[None, :]
    to_request = matches.astype(jnp.float32)
    attn_slot = jnp.dot(
        matches.T.astype(jnp.bfloat16), attn_in, preferred_element_type=jnp.float32
    ).astype(jnp.bfloat16)
    slot_len = jnp.sum(jnp.where(matches, lengths[:, None], 0), axis=0)
    my_len = lax.dynamic_slice_in_dim(slot_len, lax.axis_index("gx") * rows_dev, rows_dev, 0)
    qkv = (
        lax.psum_scatter(
            jnp.dot(attn_slot, w_qkv, preferred_element_type=jnp.float32),
            "gx",
            scatter_dimension=0,
            tiled=True,
        )
        + b_qkv
    )
    qkv = qkv.reshape(rows_dev, heads_dev, 3, HD)
    position = my_len - 1
    query = rotate(qkv[:, :, 0], position).astype(jnp.bfloat16)
    new_key = rotate(qkv[:, :, 1], position).astype(jnp.bfloat16)
    new_value = qkv[:, :, 2].astype(jnp.bfloat16)
    new_keys = key_cache
    new_values = value_cache
    zero_index = jnp.int32(0)
    for local_slot in range(rows_dev):
        slot_index = jnp.int32(local_slot)
        new_keys = lax.dynamic_update_slice(
            new_keys,
            new_key[local_slot][None, :, None, :],
            (slot_index, zero_index, position[local_slot], zero_index),
        )
        new_values = lax.dynamic_update_slice(
            new_values,
            new_value[local_slot][None, :, None, :],
            (slot_index, zero_index, position[local_slot], zero_index),
        )
    scores, valid = block_scores(query, new_keys, my_len)
    top_score = jnp.max(scores, axis=2)
    weights = jnp.where(valid, jnp.exp(scores - top_score[:, :, None]), 0.0)
    total = jnp.sum(weights, axis=2)
    weights_low = weights.astype(jnp.bfloat16)
    weighted = jnp.einsum(
        "shp,shpd->shd", weights_low, new_values, preferred_element_type=jnp.float32
    )
    attended = (weighted / total[:, :, None]).astype(jnp.bfloat16).reshape(rows_dev, heads_dev * HD)
    slot_part = jnp.dot(
        lax.all_gather(attended, "gx", axis=0, tiled=True),
        w_out,
        preferred_element_type=jnp.float32,
    )
    attn_part = jnp.dot(to_request, slot_part, precision=lax.Precision.HIGHEST)
    up_partial = jnp.dot(mlp_in, w_up, preferred_element_type=jnp.float32)
    up = lax.psum(up_partial, "gx") + b_up
    hidden = jax.nn.gelu(up, approximate=False).astype(jnp.bfloat16)
    mlp_part = jnp.dot(hidden, w_down, preferred_element_type=jnp.float32)
    branches = lax.psum(attn_part + mlp_part, "gy")
    hidden_out = (wide_in + branches + b_out + b_down).astype(jnp.bfloat16)
    return (hidden_out, new_keys, new_values)


def solution(mesh):
    return jax.shard_map(
        on_device,
        mesh=mesh,
        in_specs=(
            P(None, "gx"),
            P("gx"),
            P("gx"),
            P("gx"),
            P("gx"),
            P("gx", "gy"),
            P("gy"),
            P("gy", "gx"),
            P("gx"),
            P("gx", "gy"),
            P("gy"),
            P("gy", "gx"),
            P("gx"),
            P("gx", "gy", None, None),
            P("gx", "gy", None, None),
            P(),
            P(),
        ),
        out_specs=(P(None, "gx"), P("gx", "gy", None, None), P("gx", "gy", None, None)),
        check_vma=False,
    )
```

profile of v0, /device:TPU:2, one launch (start us, length us, event | category | flops | bytes accessed | tf_op | source)
XLA Modules:
  0.0 324.9 jit_solution(3638242814341928627)
XLA Ops:
  7.2 0.0 copy-start
  7.2 0.0 copy-start.3
  7.2 0.0 all-reduce.5.cloned.1.call-start
  7.2 1.8 copy-done.3
  9.0 0.0 copy-start.9
  9.0 0.0 copy-start.10
  9.0 1.5 copy.66
  10.5 0.0 copy-done.4
  10.5 0.1 convert_reduce_fusion
  10.7 73.7 %all-reduce.1 = (f32[64]{0:T(128)S(1)}, f32[64]{0:T(128)S(1)}) all-reduce(f32[64]{0:T(128)S(1)} %get-tuple-element.4, f32[64]{0:T(128)S(1)} %get-tuple-element.3), channel_id=1, replica_groups=mesh['gx'=32,'gy'=8] {'gx'}, use_global_device_ids=true, to_apply=%region_4.5 | all-reduce | flops 128 | bytes 1024 | tf_op jit(solution)/shard_map/psum | solution.py:62
  84.4 1.2 fusion.61
  85.5 0.0 copy-done.10
  85.5 2.5 fusion.4
  88.0 0.0 all-reduce.5.cloned.1.call-update
  88.1 0.0 copy-done.13
  88.1 0.1 select_reduce_fusion
  88.2 0.1 fusion.118
  88.3 0.6 fusion.122
  91.5 0.6 dynamic-slice
  94.1 0.1 multiply_cosine_fusion
  94.2 0.1 iota_compare_fusion.4
  94.3 142.2 %all-reduce.5.cloned.1.call-done = (f32[64,1920]{1,0:T(8,128)}, f32[64,2560]{1,0:T(8,128)}) async-done(((f32[64,1920]{1,0:T(8,128)}, f32[64,2560]{1,0:T(8,128)}), (f32[64,1920]{1,0:T(8,128)}, f32[64,2560]{1,0:T(8,128)})) %all-reduce.5.cloned.1.call-update) | async-done | bytes 1146896
  236.5 0.8 dynamic-slice_add_fusion
  237.4 0.1 slice.90
  237.5 0.1 slice.91
  237.5 0.1 subtract_convert_fusion.1
  237.6 0.1 pad_maximum_fusion
  237.7 1.3 dynamic_update_slice.12
  239.1 0.1 maximum_bitcast_fusion
  239.1 1.3 dynamic_update_slice.13
  240.5 2.5 fusion.84
  243.0 0.1 fusion.3
  243.1 0.1 fusion.119
  243.2 0.1 copy.42
  243.3 0.0 copy-done.2
  243.4 0.0 copy-start.1
  243.4 0.4 fusion.59
  243.8 0.1 fusion.83
  243.9 0.9 reshape.113
  244.8 41.8 %all-gather = bf16[32,2,640]{2,1,0:T(2,128)(2,1)S(1)} all-gather(bf16[1,2,640]{2,1,0:T(2,128)(2,1)} %reshape.113), channel_id=1, replica_groups=mesh['gx'=32,'gy'=8] {'gx'}, dimensions={0}, use_global_device_ids=true | all-gather | bytes 84480 | tf_op jit(solution)/shard_map/all_gather | solution.py:117
  286.6 0.7 reshape.114
  287.3 1.1 fusion.123
  288.5 0.9 fusion.77
  289.3 0.0 copy-start.11
  289.4 0.0 copy-start.12
  289.4 3.5 %convolution_add_fusion = f32[64,160]{1,0:T(8,128)} fusion(f32[64,160]{1,0:T(8,128)S(1)} %fusion.77, bf16[2560,160]{0,1:T(8,128)(2,1)} %param.28, f32[64,2560]{1,0:T(8,128)} %get-tuple-element.8, f32[2560]{0:T(1024)} %param.27), kind=kOutput, calls=%fused_computation.1 | convolution fusion | flops 63252480 | bytes 1566720 | tf_op jit(solution)/shard_map/dot_general | solution.py:125
  292.9 24.5 %psum.31 = f32[64,160]{1,0:T(8,128)S(1)} all-reduce(f32[64,160]{1,0:T(8,128)} %convolution_add_fusion), channel_id=1, replica_groups=mesh['gx'=32,'gy'=8] {'gy'}, use_global_device_ids=true, to_apply=%region_9.10 | all-reduce | flops 10240 | bytes 81920 | tf_op jit(solution)/shard_map/psum | solution.py:126
  317.4 0.6 fusion.57
  (29 shorter events, 0.2 us)
Async XLA Ops:
  7.2 77.2 %copy-start = (bf16[160,2560]{1,0:T(8,128)(2,1)S(1)}, bf16[160,2560]{1,0:T(8,128)(2,1)}, u32[]{:S(2)}) copy-start(bf16[160,2560]{1,0:T(8,128)(2,1)} %param.26) | copy-start | bytes 2457604
  7.2 1.8 copy-start.3
  7.2 229.3 %all-reduce.5.cloned.1.call-start = ((), (), s32[]{:S(2)}) async-start(), calls=%async_computation | async-start | bytes 2293760
  9.0 1.5 copy-start.4
  9.0 75.4 %copy-start.7 = (f32[160]{0:T(256)S(1)}, f32[160]{0:T(256)}, u32[]{:S(2)}) copy-start(f32[160]{0:T(256)} %param.21) | copy-start | bytes 1924
  9.0 75.4 %copy-start.8 = (f32[160]{0:T(256)S(1)}, f32[160]{0:T(256)}, u32[]{:S(2)}) copy-start(f32[160]{0:T(256)} %param.20) | copy-start | bytes 1924
  9.0 76.5 %copy-start.6 = (s32[64]{0:T(128)S(1)}, s32[64]{0:T(128)}, u32[]{:S(2)}) copy-start(s32[64]{0:T(128)} %param.33) | copy-start | bytes 772
  9.0 76.5 %copy-start.9 = (f32[160]{0:T(256)S(1)}, f32[160]{0:T(256)}, u32[]{:S(2)}) copy-start(f32[160]{0:T(256)} %param.19) | copy-start | bytes 1924
  9.0 76.5 %copy-start.10 = (f32[160]{0:T(256)S(1)}, f32[160]{0:T(256)}, u32[]{:S(2)}) copy-start(f32[160]{0:T(256)} %param.18) | copy-start | bytes 1924
  10.5 77.6 %copy-start.13 = (s32[64]{0:T(128)S(1)}, s32[64]{0:T(128)}, u32[]{:S(2)}) copy-start(s32[64]{0:T(128)} %param.32) | copy-start | bytes 772
  10.5 81.0 %copy-start.14 = (u32[256]{0:T(256)S(1)}, u32[256]{0:T(256)}, u32[]{:S(2)}) copy-start(u32[256]{0:T(256)} %constant.103) | copy-start | bytes 3076
  10.5 225.9 %copy-start.5 = (f32[1920]{0:T(1024)S(1)}, f32[1920]{0:T(1024)}, u32[]{:S(2)}) copy-start(f32[1920]{0:T(1024)} %param.23) | copy-start | bytes 23044
  85.5 157.8 %copy-start.2 = (bf16[2,5,1024,128]{3,2,1,0:T(8,128)(2,1)S(1)}, bf16[2,5,1024,128]{3,2,1,0:T(8,128)(2,1)}, u32[]{:S(2)}) copy-start(bf16[2,5,1024,128]{3,2,1,0:T(8,128)(2,1)} %param.31) | copy-start | bytes 7864324
  243.4 49.5 %copy-start.1 = (bf16[2,5,1024,128]{3,2,1,0:T(8,128)(2,1)}, bf16[2,5,1024,128]{3,2,1,0:T(8,128)(2,1)S(1)}, u32[]{:S(2)}) copy-start(bf16[2,5,1024,128]{3,2,1,0:T(8,128)(2,1)S(1)} %dynamic_update_slice.15) | copy-start | bytes 7864324
  289.3 28.1 %copy-start.11 = (f32[160]{0:T(256)S(1)}, f32[160]{0:T(256)}, u32[]{:S(2)}) copy-start(f32[160]{0:T(256)} %param.29) | copy-start | bytes 1924
  289.4 28.1 %copy-start.12 = (f32[160]{0:T(256)S(1)}, f32[160]{0:T(256)}, u32[]{:S(2)}) copy-start(f32[160]{0:T(256)} %param.25) | copy-start | bytes 1924
Sparse Core Ops, SparseCore 0:
  88.2 148.2 all-reduce.4
where the time goes:
time: 325 us
  waiting for transfers between devices  142 us (44%)
  blocking collectives  140 us (43%)
  between operations  18.9 us (6%)
  matrix products  12.2 us (4%)
  local copies, waits for them, and re-layouts  9.11 us (3%)
    unnamed x2, waiting for transfers between devices  142 us
    psum x1, blocking collectives, on_device(): lax.psum((jnp.sum(wide_in, axis=1), jnp.sum(wide_in * wide_in, axis=1)),...  73.7 us
    all_gather x1, blocking collectives, on_device(): lax.all_gather(attended, 'gx', axis=0, tiled=True)  41.8 us
    psum x1, blocking collectives, on_device(): branches = lax.psum(attn_part + mlp_part, 'gy')  24.5 us
  transfers between devices with their start and end apart: 1, of which 1 were waited for; matrix products, arithmetic and copies ran while one was open for 0% of the time, Pallas kernels for 0%

commit v1 on v0

--- a/solution.py
+++ b/solution.py
@@ -6,6 +6,12 @@
 D = 5120
 HD = 128
 ROT = 32
+
+
+def gather_from_all(x, axis, dim):
+    size = lax.axis_size(axis)
+    repeats = [size if d == dim else 1 for d in range(x.ndim)]
+    return lax.all_to_all(jnp.tile(x, repeats), axis, split_axis=dim, concat_axis=dim, tiled=True)
 
 
 def rotate(tensor, position):
@@ -114,9 +120,7 @@
     )
     attended = (weighted / total[:, :, None]).astype(jnp.bfloat16).reshape(rows_dev, heads_dev * HD)
     slot_part = jnp.dot(
-        lax.all_gather(attended, "gx", axis=0, tiled=True),
-        w_out,
-        preferred_element_type=jnp.float32,
+        gather_from_all(attended, "gx", 0), w_out, preferred_element_type=jnp.float32
     )
     attn_part = jnp.dot(to_request, slot_part, precision=lax.Precision.HIGHEST)
     up_partial = jnp.dot(mlp_in, w_up, preferred_element_type=jnp.float32)

time: 325 us -> 299 us (0.920)
  blocking collectives: 140 us -> 114 us
    all_gather x1 -> x0, blocking collectives: 41.8 us -> none  [on_device(): lax.all_gather(attended, 'gx', axis=0, tiled=True)]
    all_to_all x0 -> x1, blocking collectives: none -> 16 us  [gather_from_all(): lax.all_to_all(jnp.tile(x, repeats), axis, split_axis=dim, concat_axis=di...]
  transfers between devices with their start and end apart: 1 -> 1, of which waited for: 1 -> 1; matrix products, arithmetic and copies ran while one was open for 0% -> 1% of each run, Pallas kernels for 0% -> 0%
where the time goes in v1:
time: 299 us; the launch traced here: 298 us
  waiting for transfers between devices  142 us (47%)
  blocking collectives  114 us (38%)
  between operations  18.9 us (6%)
  matrix products  12.2 us (4%)
  local copies, waits for them, and re-layouts  8.26 us (3%)
    unnamed x2, waiting for transfers between devices  142 us
    psum x1, blocking collectives, on_device(): lax.psum((jnp.sum(wide_in, axis=1), jnp.sum(wide_in * wide_in, axis=1)),...  73.7 us
    psum x1, blocking collectives, on_device(): branches = lax.psum(attn_part + mlp_part, 'gy')  24.5 us
    all_to_all x1, blocking collectives, gather_from_all(): lax.all_to_all(jnp.tile(x, repeats), axis, split_axis=dim, concat_axis=di...  16 us
  transfers between devices with their start and end apart: 1, of which 1 were waited for; matrix products, arithmetic and copies ran while one was open for 1% of the time, Pallas kernels for 0%

profile of v1, /device:TPU:2, one launch (start us, length us, event | category | flops | bytes accessed | tf_op | source)
XLA Modules:
  0.0 298.2 jit_solution(8507129718702844701)
XLA Ops:
  7.2 0.0 copy-start
  7.2 0.0 copy-start.3
  7.2 0.0 all-reduce.5.cloned.1.call-start
  7.2 1.8 copy-done.3
  9.0 0.0 copy-start.9
  9.0 0.0 copy-start.10
  9.0 1.5 copy.71
  10.5 0.0 copy-done.4
  10.5 0.1 convert_reduce_fusion
  10.7 73.7 %all-reduce.1 = (f32[64]{0:T(128)S(1)}, f32[64]{0:T(128)S(1)}) all-reduce(f32[64]{0:T(128)S(1)} %get-tuple-element.4, f32[64]{0:T(128)S(1)} %get-tuple-element.3), channel_id=1, replica_groups=mesh['gx'=32,'gy'=8] {'gx'}, use_global_device_ids=true, to_apply=%region_4.5 | all-reduce | flops 128 | bytes 1024 | tf_op jit(solution)/shard_map/psum | solution.py:68
  84.4 0.0 copy-done
  84.4 1.2 fusion.61
  85.5 0.0 copy-done.10
  85.5 2.5 fusion.4
  88.0 0.0 all-reduce.5.cloned.1.call-update
  88.1 0.0 copy-done.13
  88.1 0.1 select_reduce_fusion
  88.2 0.1 broadcast_add_fusion
  88.3 0.6 fusion.122
  91.5 0.6 dynamic-slice
  94.1 0.1 multiply_cosine_fusion
  94.2 0.1 iota_compare_fusion.4
  94.3 142.2 %all-reduce.5.cloned.1.call-done = (f32[64,1920]{1,0:T(8,128)}, f32[64,2560]{1,0:T(8,128)}) async-done(((f32[64,1920]{1,0:T(8,128)}, f32[64,2560]{1,0:T(8,128)}), (f32[64,1920]{1,0:T(8,128)}, f32[64,2560]{1,0:T(8,128)})) %all-reduce.5.cloned.1.call-update) | async-done | bytes 1146896
  236.5 0.8 dynamic-slice_add_fusion
  237.4 0.1 slice.91
  237.5 0.1 slice.90
  237.5 0.1 subtract_convert_fusion.1
  237.6 0.1 pad_maximum_fusion
  237.7 0.1 maximum_bitcast_fusion
  237.8 1.3 dynamic_update_slice.12
  239.1 1.3 dynamic_update_slice.13
  240.5 2.5 fusion.84
  243.0 0.1 fusion.3
  243.1 0.1 convert_bitcast_fusion
  243.2 0.1 copy.42
  243.4 0.0 copy-start.1
  243.4 0.4 fusion.59
  243.8 0.1 fusion.86
  243.9 0.1 tile.9
  244.0 16.0 %all_to_all.9 = bf16[32,2,640]{2,1,0:T(2,128)(2,1)S(1)} all-to-all(bf16[32,2,640]{2,1,0:T(2,128)(2,1)S(1)} %tile.9), channel_id=1, replica_groups=mesh['gx'=32,'gy'=8] {'gx'}, dimensions={0} | all-to-all | bytes 163840 | tf_op jit(solution)/shard_map/all_to_all | solution.py:14
  259.9 0.7 all_to_all.7
  260.6 1.2 fusion.123
  261.8 0.9 fusion.77
  262.7 0.0 copy-start.11
  262.7 0.0 copy-start.12
  262.7 3.5 %convolution_add_fusion = f32[64,160]{1,0:T(8,128)} fusion(f32[64,160]{1,0:T(8,128)S(1)} %fusion.77, bf16[2560,160]{0,1:T(8,128)(2,1)} %param.28, f32[64,2560]{1,0:T(8,128)} %get-tuple-element.8, f32[2560]{0:T(1024)} %param.27), kind=kOutput, calls=%fused_computation.1 | convolution fusion | flops 63252480 | bytes 1566720 | tf_op jit(solution)/shard_map/dot_general | solution.py:129
  266.3 24.5 %psum.31 = f32[64,160]{1,0:T(8,128)S(1)} all-reduce(f32[64,160]{1,0:T(8,128)} %convolution_add_fusion), channel_id=1, replica_groups=mesh['gx'=32,'gy'=8] {'gy'}, use_global_device_ids=true, to_apply=%region_9.10 | all-reduce | flops 10240 | bytes 81920 | tf_op jit(solution)/shard_map/psum | solution.py:130
  290.8 0.6 fusion.57
  (30 shorter events, 0.2 us)
Async XLA Ops:
  7.2 77.2 %copy-start = (bf16[160,2560]{1,0:T(8,128)(2,1)S(1)}, bf16[160,2560]{1,0:T(8,128)(2,1)}, u32[]{:S(2)}) copy-start(bf16[160,2560]{1,0:T(8,128)(2,1)} %param.26) | copy-start | bytes 2457604
  7.2 1.8 copy-start.3
  7.2 229.3 %all-reduce.5.cloned.1.call-start = ((), (), s32[]{:S(2)}) async-start(), calls=%async_computation.1 | async-start | bytes 2293760
  9.0 1.5 copy-start.4
  9.0 75.4 %copy-start.7 = (f32[160]{0:T(256)S(1)}, f32[160]{0:T(256)}, u32[]{:S(2)}) copy-start(f32[160]{0:T(256)} %param.21) | copy-start | bytes 1924
  9.0 75.4 %copy-start.8 = (f32[160]{0:T(256)S(1)}, f32[160]{0:T(256)}, u32[]{:S(2)}) copy-start(f32[160]{0:T(256)} %param.20) | copy-start | bytes 1924
  9.0 76.5 %copy-start.6 = (s32[64]{0:T(128)S(1)}, s32[64]{0:T(128)}, u32[]{:S(2)}) copy-start(s32[64]{0:T(128)} %param.33) | copy-start | bytes 772
  9.0 76.5 %copy-start.9 = (f32[160]{0:T(256)S(1)}, f32[160]{0:T(256)}, u32[]{:S(2)}) copy-start(f32[160]{0:T(256)} %param.19) | copy-start | bytes 1924
  9.0 76.5 %copy-start.10 = (f32[160]{0:T(256)S(1)}, f32[160]{0:T(256)}, u32[]{:S(2)}) copy-start(f32[160]{0:T(256)} %param.18) | copy-start | bytes 1924
  10.5 77.6 %copy-start.13 = (s32[64]{0:T(128)S(1)}, s32[64]{0:T(128)}, u32[]{:S(2)}) copy-start(s32[64]{0:T(128)} %param.32) | copy-start | bytes 772
  10.5 81.0 %copy-start.14 = (u32[256]{0:T(256)S(1)}, u32[256]{0:T(256)}, u32[]{:S(2)}) copy-start(u32[256]{0:T(256)} %constant.103) | copy-start | bytes 3076
  10.5 225.9 %copy-start.5 = (f32[1920]{0:T(1024)S(1)}, f32[1920]{0:T(1024)}, u32[]{:S(2)}) copy-start(f32[1920]{0:T(1024)} %param.23) | copy-start | bytes 23044
  85.5 157.8 %copy-start.2 = (bf16[2,5,1024,128]{3,2,1,0:T(8,128)(2,1)S(1)}, bf16[2,5,1024,128]{3,2,1,0:T(8,128)(2,1)}, u32[]{:S(2)}) copy-start(bf16[2,5,1024,128]{3,2,1,0:T(8,128)(2,1)} %param.31) | copy-start | bytes 7864324
  243.4 22.9 %copy-start.1 = (bf16[2,5,1024,128]{3,2,1,0:T(8,128)(2,1)}, bf16[2,5,1024,128]{3,2,1,0:T(8,128)(2,1)S(1)}, u32[]{:S(2)}) copy-start(bf16[2,5,1024,128]{3,2,1,0:T(8,128)(2,1)S(1)} %dynamic_update_slice.15) | copy-start | bytes 7864324
  262.7 28.1 %copy-start.11 = (f32[160]{0:T(256)S(1)}, f32[160]{0:T(256)}, u32[]{:S(2)}) copy-start(f32[160]{0:T(256)} %param.29) | copy-start | bytes 1924
  262.7 28.1 %copy-start.12 = (f32[160]{0:T(256)S(1)}, f32[160]{0:T(256)}, u32[]{:S(2)}) copy-start(f32[160]{0:T(256)} %param.25) | copy-start | bytes 1924
Sparse Core Ops, SparseCore 0:
  88.2 148.2 all-reduce.4
